TPU v7x, 32 devices: a whole 2x2x4 slice. The times are simulated.
32 devices in a mesh: parts: 2 (over y), tm: 4 (over x, core), cols: 4 (over z).
Axes of the slice: x: 2, y: 2, z: 4, core: 2. Of those that a mesh axis runs over, the one named last changes fastest.
Arguments:
- noise: float32 [16, 1024, 1024], P(('parts', 'tm'), None, 'cols'), parts along dimension 0, may hold values from -6 to 6
- inv_diag: float32 [16, 1024, 1024], P(('parts', 'tm'), None, 'cols'), parts along dimension 0, may hold values from -2 to 2, as said below
- coupling: float32 [16, 1024, 1024], P(('parts', 'tm'), None, 'cols'), parts along dimension 0, may hold values from -1 to 1, as said below
- order: int32 [1024], replicated, may hold values from 0 to 1023, each once
Outputs:
- sample: float32 [16, 1024, 1024], P(('parts', 'tm'), None, 'cols'), parts along dimension 0
There are 2 independent parts, one for each index of `parts`. A program takes and returns all parts, laid end to end along the dimension named above; an argument that names none is the same for every part. Nothing has to cross between parts.
Inputs may be any that keep to these rules, and one draw needn't show every extreme that they name: `order`: each of 0 to 1023 appears once. `inv_diag`: diagonal entries lie between 0.5 and 2, off-diagonal entries are small in magnitude. `coupling`: diagonal entries lie between 0.5 and 0.97, off-diagonal entries are small in magnitude.
All inputs are finite; a program needn't handle non-finite values.
Results may differ from a plain program's by a relative error of at most 0.00013.
Values sent between devices are 32-bit elements; how exact they have to be, the bound alone decides.
No kernel may reach another device: no remote copies, remote signals or barrier semaphores. Data moves between devices by JAX's collectives and lax.ppermute only.
A program may use at most 128 MiB of HBM per device.

v0:
```python
import jax
import jax.numpy as jnp
from jax import lax
from jax.sharding import PartitionSpec as P

low = jnp.bfloat16


def shifted(block, axis, distance):
    devices = range(lax.axis_size(axis))
    route = [(i - distance, i) for i in devices if i - distance in devices]
    return lax.ppermute(block, axis, route)


def split(value, count):
    parts = []
    rest = value
    for index in range(count):
        kept = lax.reduce_precision(rest, exponent_bits=8, mantissa_bits=7)
        parts.append(kept.astype(low))
        if index < count - 1:
            rest = rest - kept
    return parts


def bdot(left, right):
    return jnp.dot(left, right, preferred_element_type=jnp.float32)


def apply(matrix_parts, operand):
    high, small = matrix_parts
    operand_high, operand_small = split(operand, 2)
    return bdot(high, operand_high) + (bdot(high, operand_small) + bdot(small, operand_high))


def shards(noise, inv_diag, coupling, order):
    block_count = noise.shape[0]
    node_count = noise.shape[1]
    sample_count = noise.shape[2]
    pieces = 2 if sample_count % 256 == 0 else 1
    width = sample_count // pieces
    inv_full = lax.all_gather(inv_diag, "cols", axis=2, tiled=True)
    coupling_parts = [
        split(lax.all_gather(coupling[block], "cols", axis=1, tiled=True), 2)
        for block in range(block_count)
    ]
    driven = [apply(split(inv_full[block], 2), noise[block]) for block in range(block_count)]
    driven_pieces = [
        [driven[block][:, p * width : (p + 1) * width] for p in range(pieces)]
        for block in range(block_count)
    ]

    def chain(entering, piece, skip_last):
        carried = entering
        results = [None] * block_count
        for block in range(block_count - 1, -1, -1):
            if skip_last and block == block_count - 1:
                carried = driven_pieces[block][piece]
            else:
                carried = driven_pieces[block][piece] + apply(coupling_parts[block], carried)
            results[block] = carried
        return results

    first = [shifted(chain(None, p, True)[0], "tm", -1) for p in range(pieces)]

    def relay_step(step, entering):
        return [shifted(chain(entering[p], p, False)[0], "tm", -1) for p in range(pieces)]

    entering = lax.fori_loop(0, lax.axis_size("tm") - 2, relay_step, first)
    finals = [chain(entering[p], p, False) for p in range(pieces)]
    selector = (order[:, None] == jnp.arange(node_count, dtype=order.dtype)[None, :]).astype(low)
    outputs = []
    for block in range(block_count):
        field = jnp.concatenate([finals[p][block] for p in range(pieces)], axis=1)
        top, middle, bottom = split(field, 3)
        outputs.append(bdot(selector, top) + (bdot(selector, middle) + bdot(selector, bottom)))
    return jnp.stack(outputs, axis=0)


def solution(mesh):
    return jax.shard_map(
        shards,
        mesh=mesh,
        in_specs=(
            P(("parts", "tm"), None, "cols"),
            P(("parts", "tm"), None, "cols"),
            P(("parts", "tm"), None, "cols"),
            P(),
        ),
        out_specs=P(("parts", "tm"), None, "cols"),
        check_vma=False,
    )
```

profile of v0, /device:TPU:1, one launch (start us, length us, event | category | flops | bytes accessed | tf_op | source)
XLA Modules:
  0.0 439.5 jit_solution(6839977181822519246)
XLA Ops:
  6.5 3.0 fusion.150
  11.0 81.5 %all-gather.8.cloned.1.call-done = f32[1,1024,1024]{2,1,0:T(8,128)} async-done(((f32[1,1024,256]{2,1,0:T(8,128)}), f32[1,1024,1024]{2,1,0:T(8,128)}) %all-gather.8.cloned.1.call-update) | async-done | bytes 4194320 | tf_op jit(solution)/shard_map/all_gather | solution.py:44
  92.6 4.4 %reduce-precision_convert_fusion.13 = (bf16[1024,1024]{1,0:T(8,128)(2,1)S(1)}, bf16[1024,1024]{1,0:T(8,128)(2,1)}) fusion(f32[1,1024,1024]{2,1,0:T(8,128)} %all-gather.8.cloned.1.call-done), kind=kLoop, calls=%fused_computation.43 | loop fusion | flops 5242880 | bytes 8388608 | tf_op jit(solution)/shard_map/convert_element_type | solution.py:20
  97.0 76.5 %all-gather.10.cloned.1.call-done = f32[1,1024,1024]{2,1,0:T(8,128)} async-done(((f32[1,1024,256]{2,1,0:T(8,128)}), f32[1,1024,1024]{2,1,0:T(8,128)}) %all-gather.10.cloned.1.call-update) | async-done | bytes 4194320 | tf_op jit(solution)/shard_map/all_gather | solution.py:44
  173.5 5.0 %reduce-precision_convert_fusion.12 = (bf16[1024,1024]{1,0:T(8,128)(2,1)}, bf16[1024,1024]{1,0:T(8,128)(2,1)}) fusion(f32[1,1024,1024]{2,1,0:T(8,128)} %all-gather.10.cloned.1.call-done), kind=kLoop, calls=%fused_computation.41 | loop fusion | flops 5242880 | bytes 8388608 | tf_op jit(solution)/shard_map/convert_element_type | solution.py:20
  178.5 144.9 %all-gather.6.cloned.1.call-done = f32[2,1024,1024]{2,1,0:T(8,128)} async-done(((f32[2,1024,256]{2,1,0:T(8,128)}), f32[2,1024,1024]{2,1,0:T(8,128)}) %all-gather.6.cloned.1.call-update) | async-done | bytes 8388624 | tf_op jit(solution)/shard_map/all_gather | solution.py:42
  323.4 3.4 fusion.47
  326.9 3.8 fusion.97
  338.1 1.7 fusion.74
  339.8 1.7 fusion.71
  341.5 2.4 collective-permute-start.2
  343.8 2.1 collective-permute-start.3
  345.9 1.1 fusion.152
  347.0 2.0 copy.10
  349.0 2.0 copy.9
  351.1 2.3 fusion.151
  353.4 4.4 %collective-permute-done.3 = f32[1024,128]{0,1:T(8,128)S(1)} collective-permute-done((f32[1024,128]{0,1:T(8,128)}, f32[1024,128]{0,1:T(8,128)S(1)}, u32[]{:S(2)}, u32[]{:S(2)}) %collective-permute-start.3) | collective-permute-done | bytes 524320 | tf_op jit(solution)/shard_map/ppermute | solution.py:12
  357.8 54.2 %while.12 = (s32[]{:T(128)}, f32[1024,128]{0,1:T(8,128)S(1)}, f32[1024,128]{0,1:T(8,128)S(1)}, bf16[1024,1024]{1,0:T(8,128)(2,1)}, bf16[1024,1024]{1,0:T(8,128)(...) while((s32[]{:T(128)}, f32[1024,128]{0,1:T(8,128)S(1)}, ...), condition=%wide.region_1.0_spmd, body=%wide.region_0.0_spmd.sunk | while | flops 3226992640 | bytes 81789320 | solution.py:69
  357.8 2.5 fusion.228
  364.5 1.7 fusion.232
  366.2 1.9 collective-permute-start
  372.5 1.7 fusion.238
  374.2 1.9 collective-permute-start.1
  376.9 8.0 %collective-permute-done.1 = f32[1024,128]{0,1:T(8,128)S(1)} collective-permute-done((f32[1024,128]{0,1:T(8,128)}, f32[1024,128]{0,1:T(8,128)S(1)}, u32[]{:S(2)}, u32[]{:S(2)}) %collective-permute-start.1) | collective-permute-done | bytes 524320 | tf_op jit(solution)/shard_map/while/body/eval_jaxpr/ppermute | solution.py:12
  384.9 2.5 fusion.228
  391.7 1.7 fusion.232
  393.3 1.9 collective-permute-start
  399.7 1.7 fusion.238
  401.3 1.9 collective-permute-start.1
  404.0 8.0 %collective-permute-done.1 = f32[1024,128]{0,1:T(8,128)S(1)} collective-permute-done((f32[1024,128]{0,1:T(8,128)}, f32[1024,128]{0,1:T(8,128)S(1)}, u32[]{:S(2)}, u32[]{:S(2)}) %collective-permute-start.1) | collective-permute-done | bytes 524320 | tf_op jit(solution)/shard_map/while/body/eval_jaxpr/ppermute | solution.py:12
  412.0 2.6 fusion.136
  431.5 1.5 pad_maximum_fusion
  (102 shorter events, 44.3 us)
Async XLA Ops:
  6.5 86.0 %all-gather.8.cloned.1.call-start = ((), (), s32[]{:S(2)}) async-start(), calls=%async_computation.1 | async-start | bytes 5242880 | tf_op jit(solution)/shard_map/all_gather | solution.py:44
  9.6 163.9 %all-gather.10.cloned.1.call-start = ((), (), s32[]{:S(2)}) async-start(), calls=%async_computation.2 | async-start | bytes 5242880 | tf_op jit(solution)/shard_map/all_gather | solution.py:44
  10.3 313.1 %all-gather.6.cloned.1.call-start = ((), (), s32[]{:S(2)}) async-start(), calls=%async_computation | async-start | bytes 10485760 | tf_op jit(solution)/shard_map/all_gather | solution.py:42
  323.4 7.2 %copy-start.7 = (f32[2,1024,1024]{2,1,0:T(8,128)S(1)}, f32[2,1024,1024]{2,1,0:T(8,128)}, u32[]{:S(2)}) copy-start(f32[2,1024,1024]{2,1,0:T(8,128)} %all-gather.6.cloned.1.call-done) | copy-start | bytes 25165828
  326.8 4.0 copy-start.14
  330.8 1.6 copy-start.2
  331.6 14.3 %copy-start.8 = (f32[1024,256]{0,1:T(8,128)}, f32[1024,256]{0,1:T(8,128)S(1)}, u32[]{:S(2)}) copy-start(f32[1024,256]{0,1:T(8,128)S(1)} %fusion.69) | copy-start | bytes 3145732
  338.1 1.7 copy-start.15
  341.5 11.9 %collective-permute-start.2 = (f32[1024,128]{0,1:T(8,128)}, f32[1024,128]{0,1:T(8,128)S(1)}, u32[]{:S(2)}, u32[]{:S(2)}) collective-permute-start(f32[1024,128]{0,1:T(8,128)} %fusion.71), channel_id=1, source_target_pairs={{4,0},{8,4},{12,8},{5,1},{9,5},{13,9},{6,2},{10,6},{14,10},{7,3},{... | collective-permute-start | bytes 1572872 | tf_op jit(solution)/shard_map/ppermute | solution.py:12
  343.8 14.0 %collective-permute-start.3 = (f32[1024,128]{0,1:T(8,128)}, f32[1024,128]{0,1:T(8,128)S(1)}, u32[]{:S(2)}, u32[]{:S(2)}) collective-permute-start(f32[1024,128]{0,1:T(8,128)} %fusion.74), channel_id=1, source_target_pairs={{4,0},{8,4},{12,8},{5,1},{9,5},{13,9},{6,2},{10,6},{14,10},{7,3},{... | collective-permute-start | bytes 1572872 | tf_op jit(solution)/shard_map/ppermute | solution.py:12
  357.8 2.5 copy-start
  360.2 1.0 copy-start.11
  362.9 1.6 copy-start.3
  362.9 1.7 copy-start.13
  364.5 3.6 copy-start.5
  366.2 10.7 %collective-permute-start = (f32[1024,128]{0,1:T(8,128)}, f32[1024,128]{0,1:T(8,128)S(1)}, u32[]{:S(2)}, u32[]{:S(2)}) collective-permute-start(f32[1024,128]{0,1:T(8,128)} %fusion.232), channel_id=1, source_target_pairs={{4,0},{8,4},{12,8},{5,1},{9,5},{13,9},{6,2},{10,6},{14,10},{7,3},{... | collective-permute-start | bytes 1572872 | tf_op jit(solution)/shard_map/while/body/eval_jaxpr/ppermute | solution.py:12
  368.8 1.0 copy-start.10
  371.5 1.0 copy-start.12
  374.2 10.7 %collective-permute-start.1 = (f32[1024,128]{0,1:T(8,128)}, f32[1024,128]{0,1:T(8,128)S(1)}, u32[]{:S(2)}, u32[]{:S(2)}) collective-permute-start(f32[1024,128]{0,1:T(8,128)} %fusion.238), channel_id=1, source_target_pairs={{4,0},{8,4},{12,8},{5,1},{9,5},{13,9},{6,2},{10,6},{14,10},{7,3},{... | collective-permute-start | bytes 1572872 | tf_op jit(solution)/shard_map/while/body/eval_jaxpr/ppermute | solution.py:12
  384.9 2.5 copy-start
  387.4 1.0 copy-start.11
  390.0 1.6 copy-start.3
  390.0 1.7 copy-start.13
  391.6 3.6 copy-start.5
  393.3 10.7 %collective-permute-start = (f32[1024,128]{0,1:T(8,128)}, f32[1024,128]{0,1:T(8,128)S(1)}, u32[]{:S(2)}, u32[]{:S(2)}) collective-permute-start(f32[1024,128]{0,1:T(8,128)} %fusion.232), channel_id=1, source_target_pairs={{4,0},{8,4},{12,8},{5,1},{9,5},{13,9},{6,2},{10,6},{14,10},{7,3},{... | collective-permute-start | bytes 1572872 | tf_op jit(solution)/shard_map/while/body/eval_jaxpr/ppermute | solution.py:12
  398.6 1.0 copy-start.12
  401.3 10.7 %collective-permute-start.1 = (f32[1024,128]{0,1:T(8,128)}, f32[1024,128]{0,1:T(8,128)S(1)}, u32[]{:S(2)}, u32[]{:S(2)}) collective-permute-start(f32[1024,128]{0,1:T(8,128)} %fusion.238), channel_id=1, source_target_pairs={{4,0},{8,4},{12,8},{5,1},{9,5},{13,9},{6,2},{10,6},{14,10},{7,3},{... | collective-permute-start | bytes 1572872 | tf_op jit(solution)/shard_map/while/body/eval_jaxpr/ppermute | solution.py:12
  412.0 2.6 copy-start.6
  414.6 1.6 copy-start.1
  416.2 1.2 copy-start.9
  419.1 1.6 copy-start.4
  422.4 1.2 copy-start.16
  (2 other events, 1.9 us)
Sparse Core Ops, SparseCore 0:
  9.7 82.8 all-gather.7
  94.1 79.2 all-gather.9
  175.0 148.3 all-gather.5
where the time goes:
time: 440 us; the launch traced here: 439 us
  waiting for transfers between devices  326 us (74%)
  matrix products  59.5 us (14%)
  local copies, waits for them, and re-layouts  16.8 us (4%)
  between operations  13.4 us (3%)
  starting transfers between devices  12.2 us (3%)
  other arithmetic  10.9 us (2%)
    all_gather x2, waiting for transfers between devices, shards(): lax.all_gather(coupling[block], 'cols', axis=1, tiled=True)  158 us
    all_gather x1, waiting for transfers between devices, shards(): inv_full = lax.all_gather(inv_diag, 'cols', axis=2, tiled=True)  145 us
    dot_general x54, matrix products, bdot(): return jnp.dot(left, right, preferred_element_type=jnp.float32)  59.5 us
    ppermute x6, waiting for transfers between devices, shifted(): return lax.ppermute(block, axis, route)  22 us
    ppermute x6, starting transfers between devices, shifted(): return lax.ppermute(block, axis, route)  12.1 us
    convert_element_type x2, other arithmetic, split(): parts.append(kept.astype(low))  9.48 us
  transfers between devices with their start and end apart: 9, of which 8 were waited for; matrix products, arithmetic and copies ran while one was open for 6% of the time, Pallas kernels for 0%

commit v1 on v0

--- a/solution.py
+++ b/solution.py
@@ -4,6 +4,27 @@
 from jax.sharding import PartitionSpec as P
 
 low = jnp.bfloat16
+
+
+def ring_gather(x, axis, dim):
+    devices, position, extent = (lax.axis_size(axis), lax.axis_index(axis), x.shape[dim])
+    forward = [(i, (i + 1) % devices) for i in range(devices)]
+    left = [(i, (i - 1) % devices) for i in range(devices)]
+    out = jnp.zeros((*x.shape[:dim], devices * extent, *x.shape[dim + 1 :]), x.dtype)
+    out = lax.dynamic_update_slice_in_dim(out, x, position * extent, axis=dim)
+    from_left = from_right = x
+    half = devices // 2
+    for step in range(1, half + 1):
+        from_left = lax.ppermute(from_left, axis, forward)
+        out = lax.dynamic_update_slice_in_dim(
+            out, from_left, (position - step) % devices * extent, axis=dim
+        )
+        if step < devices - half:
+            from_right = lax.ppermute(from_right, axis, left)
+            out = lax.dynamic_update_slice_in_dim(
+                out, from_right, (position + step) % devices * extent, axis=dim
+            )
+    return out
 
 
 def shifted(block, axis, distance):
@@ -41,8 +62,7 @@
     width = sample_count // pieces
     inv_full = lax.all_gather(inv_diag, "cols", axis=2, tiled=True)
     coupling_parts = [
-        split(lax.all_gather(coupling[block], "cols", axis=1, tiled=True), 2)
-        for block in range(block_count)
+        split(ring_gather(coupling[block], "cols", 1), 2) for block in range(block_count)
     ]
     driven = [apply(split(inv_full[block], 2), noise[block]) for block in range(block_count)]
     driven_pieces = [

time: 440 us -> 404 us (0.918)
  waiting for transfers between devices: 326 us -> 208 us
  starting transfers between devices: 12.2 us -> 89.1 us
  local copies, waits for them, and re-layouts: 16.8 us -> 23.3 us
    ppermute x0 -> x6, waiting for transfers between devices: none -> 181 us  [the longest x4 137 us: ring_gather(): from_left = lax.ppermute(from_left, axis, forward)]
    all_gather x2 -> x0, waiting for transfers between devices: 158 us -> none  [shards(): lax.all_gather(coupling[block], 'cols', axis=1, tiled=True)]
    all_gather x1, waiting for transfers between devices: 145 us -> 6.52 us  [shards(): inv_full = lax.all_gather(inv_diag, 'cols', axis=2, tiled=True)]
    ppermute x0 -> x6, starting transfers between devices: none -> 77 us  [the longest x4 74.8 us: ring_gather(): from_left = lax.ppermute(from_left, axis, forward)]
    dynamic_update_slice x0 -> x7, local copies, waits for them, and re-layouts: none -> 4.76 us  [the longest x2 2.7 us: ring_gather(): lax.dynamic_update_slice_in_dim(out, from_right, (position + step) % devi...]
  transfers between devices with their start and end apart: 9 -> 13, of which waited for: 8 -> 11; matrix products, arithmetic and copies ran while one was open for 6% -> 8% of each run, Pallas kernels for 0% -> 0%
where the time goes in v1:
time: 404 us; the launch traced here: 400 us
  waiting for transfers between devices  208 us (51%)
  starting transfers between devices  89.1 us (22%)
  matrix products  59.4 us (15%)
  local copies, waits for them, and re-layouts  23.3 us (6%)
  between operations  13.8 us (3%)
  other arithmetic  6.7 us (2%)
    ppermute x4, waiting for transfers between devices, ring_gather(): from_left = lax.ppermute(from_left, axis, forward)  137 us
    ppermute x4, starting transfers between devices, ring_gather(): from_left = lax.ppermute(from_left, axis, forward)  74.8 us
    dot_general x54, matrix products, bdot(): return jnp.dot(left, right, preferred_element_type=jnp.float32)  59.4 us
    ppermute x2, waiting for transfers between devices, ring_gather(): from_right = lax.ppermute(from_right, axis, left)  44.3 us
    ppermute x6, waiting for transfers between devices, shifted(): return lax.ppermute(block, axis, route)  19.5 us
    ppermute x6, starting transfers between devices, shifted(): return lax.ppermute(block, axis, route)  12.1 us
  transfers between devices with their start and end apart: 13, of which 11 were waited for; matrix products, arithmetic and copies ran while one was open for 8% of the time, Pallas kernels for 0%

profile of v1, /device:TPU:1, one launch (start us, length us, event | category | flops | bytes accessed | tf_op | source)
XLA Modules:
  0.0 400.2 jit_solution(5640393190731548268)
XLA Ops:
  9.6 2.1 collective-permute-start.2
  13.0 2.0 collective-permute-start.3
  15.3 33.1 %collective-permute-done.2 = f32[1024,256]{1,0:T(8,128)S(1)} collective-permute-done((f32[1024,256]{1,0:T(8,128)}, f32[1024,256]{1,0:T(8,128)S(1)}, u32[]{:S(2)}, u32[]{:S(2)}) %collective-permute-start.2) | collective-permute-done | bytes 1048608 | tf_op jit(solution)/shard_map/ppermute | solution.py:18
  48.3 9.7 %collective-permute-start.4 = (f32[1024,256]{1,0:T(8,128)S(1)}, f32[1024,256]{1,0:T(8,128)S(1)}, u32[]{:S(2)}, u32[]{:S(2)}) collective-permute-start(f32[1024,256]{1,0:T(8,128)S(1)} %collective-permute-done.2), channel_id=1, source_target_pairs={{0,1},{1,2},{2,3},{3,0},{4,5},{5,6},{6,7},{7,4},{8,9},{9,10},{10,1... | collective-permute-start | bytes 3145736 | tf_op jit(solution)/shard_map/ppermute | solution.py:18
  58.0 35.3 %collective-permute-done.5 = f32[1024,256]{1,0:T(8,128)} collective-permute-done((f32[1024,256]{1,0:T(8,128)}, f32[1024,256]{1,0:T(8,128)}, u32[]{:S(2)}, u32[]{:S(2)}) %collective-permute-start.5) | collective-permute-done | bytes 1048608 | tf_op jit(solution)/shard_map/ppermute | solution.py:18
  93.4 61.7 %collective-permute-start.7 = (f32[1024,256]{1,0:T(8,128)}, f32[1024,256]{1,0:T(8,128)S(1)}, u32[]{:S(2)}, u32[]{:S(2)}) collective-permute-start(f32[1024,256]{1,0:T(8,128)} %collective-permute-done.5), channel_id=1, source_target_pairs={{0,1},{1,2},{2,3},{3,0},{4,5},{5,6},{6,7},{7,4},{8,9},{9,10},{10,1... | collective-permute-start | bytes 3145736 | tf_op jit(solution)/shard_map/ppermute | solution.py:18
  159.2 44.3 %collective-permute-done.6 = f32[1024,256]{1,0:T(8,128)} collective-permute-done((f32[1024,256]{1,0:T(8,128)}, f32[1024,256]{1,0:T(8,128)}, u32[]{:S(2)}, u32[]{:S(2)}) %collective-permute-start.6) | collective-permute-done | bytes 1048608 | tf_op jit(solution)/shard_map/ppermute | solution.py:23
  204.8 23.3 %collective-permute-done.4 = f32[1024,256]{1,0:T(8,128)S(1)} collective-permute-done((f32[1024,256]{1,0:T(8,128)S(1)}, f32[1024,256]{1,0:T(8,128)S(1)}, u32[]{:S(2)}, u32[]{:S(2)}) %collective-permute-start.4) | collective-permute-done | bytes 1048608 | tf_op jit(solution)/shard_map/ppermute | solution.py:18
  228.1 44.9 %collective-permute-done.7 = f32[1024,256]{1,0:T(8,128)S(1)} collective-permute-done((f32[1024,256]{1,0:T(8,128)}, f32[1024,256]{1,0:T(8,128)S(1)}, u32[]{:S(2)}, u32[]{:S(2)}) %collective-permute-start.7) | collective-permute-done | bytes 1048608 | tf_op jit(solution)/shard_map/ppermute | solution.py:18
  273.4 2.3 reduce-precision_convert_fusion.14
  275.6 3.0 reduce-precision_convert_fusion.12
  278.6 6.5 %all-gather.2.cloned.1.call-done = f32[2,1024,1024]{2,1,0:T(8,128)} async-done(((f32[2,1024,256]{2,1,0:T(8,128)}), f32[2,1024,1024]{2,1,0:T(8,128)}) %all-gather.2.cloned.1.call-update) | async-done | bytes 8388624 | tf_op jit(solution)/shard_map/all_gather | solution.py:63
  285.1 3.4 fusion.47
  288.6 3.8 fusion.85
  300.6 2.3 collective-permute-start.9
  305.5 2.1 collective-permute-start.8
  308.6 2.1 copy.13
  310.7 2.0 copy.14
  312.7 2.3 fusion.138
  315.0 1.9 collective-permute-done.8
  317.0 55.5 %while.12 = (s32[]{:T(128)}, f32[1024,128]{0,1:T(8,128)S(1)}, f32[1024,128]{0,1:T(8,128)S(1)}, bf16[1024,1024]{1,0:T(8,128)(2,1)}, bf16[1024,1024]{1,0:T(8,128)(...) while((s32[]{:T(128)}, f32[1024,128]{0,1:T(8,128)S(1)}, ...), condition=%wide.region_1.2_spmd, body=%wide.region_0.1_spmd.sunk | while | flops 3226992640 | bytes 81789320 | solution.py:89
  317.0 2.5 fusion.220
  324.3 1.7 fusion.225
  326.0 1.9 collective-permute-start.1
  334.0 1.9 collective-permute-start
  336.7 8.0 %collective-permute-done = f32[1024,128]{0,1:T(8,128)S(1)} collective-permute-done((f32[1024,128]{0,1:T(8,128)}, f32[1024,128]{0,1:T(8,128)S(1)}, u32[]{:S(2)}, u32[]{:S(2)}) %collective-permute-start) | collective-permute-done | bytes 524320 | tf_op jit(solution)/shard_map/while/body/eval_jaxpr/ppermute | solution.py:33
  344.7 2.5 fusion.220
  352.1 1.7 fusion.225
  353.8 1.9 collective-permute-start.1
  361.7 1.9 collective-permute-start
  364.5 8.0 %collective-permute-done = f32[1024,128]{0,1:T(8,128)S(1)} collective-permute-done((f32[1024,128]{0,1:T(8,128)}, f32[1024,128]{0,1:T(8,128)S(1)}, u32[]{:S(2)}, u32[]{:S(2)}) %collective-permute-start) | collective-permute-done | bytes 524320 | tf_op jit(solution)/shard_map/while/body/eval_jaxpr/ppermute | solution.py:33
  372.5 2.6 fusion.122
  (119 shorter events, 63.6 us)
Async XLA Ops:
  6.5 1.6 copy-start.17
  6.5 278.6 %all-gather.2.cloned.1.call-start = ((), (), s32[]{:S(2)}) async-start(), calls=%async_computation | async-start | bytes 10485760 | tf_op jit(solution)/shard_map/all_gather | solution.py:63
  9.6 38.7 %collective-permute-start.2 = (f32[1024,256]{1,0:T(8,128)}, f32[1024,256]{1,0:T(8,128)S(1)}, u32[]{:S(2)}, u32[]{:S(2)}) collective-permute-start(f32[1024,256]{1,0:T(8,128)} %get-tuple-element.102), channel_id=1, source_target_pairs={{0,1},{1,2},{2,3},{3,0},{4,5},{5,6},{6,7},{7,4},{8,9},{9,10},{10,1... | collective-permute-start | bytes 3145736 | tf_op jit(solution)/shard_map/ppermute | solution.py:18
  11.7 81.7 %collective-permute-start.5 = (f32[1024,256]{1,0:T(8,128)}, f32[1024,256]{1,0:T(8,128)}, u32[]{:S(2)}, u32[]{:S(2)}) collective-permute-start(f32[1024,256]{1,0:T(8,128)} %get-tuple-element.103), channel_id=1, source_target_pairs={{0,1},{1,2},{2,3},{3,0},{4,5},{5,6},{6,7},{7,4},{8,9},{9,10},{10,1... | collective-permute-start | bytes 3145736 | tf_op jit(solution)/shard_map/ppermute | solution.py:18
  13.0 144.8 %collective-permute-start.3 = (f32[1024,256]{1,0:T(8,128)}, f32[1024,256]{1,0:T(8,128)}, u32[]{:S(2)}, u32[]{:S(2)}) collective-permute-start(f32[1024,256]{1,0:T(8,128)} %get-tuple-element.102), channel_id=1, source_target_pairs={{0,3},{1,0},{2,1},{3,2},{4,7},{5,4},{6,5},{7,6},{8,11},{9,8},{10,9... | collective-permute-start | bytes 3145736 | tf_op jit(solution)/shard_map/ppermute | solution.py:23
  15.0 188.5 %collective-permute-start.6 = (f32[1024,256]{1,0:T(8,128)}, f32[1024,256]{1,0:T(8,128)}, u32[]{:S(2)}, u32[]{:S(2)}) collective-permute-start(f32[1024,256]{1,0:T(8,128)} %get-tuple-element.103), channel_id=1, source_target_pairs={{0,3},{1,0},{2,1},{3,2},{4,7},{5,4},{6,5},{7,6},{8,11},{9,8},{10,9... | collective-permute-start | bytes 3145736 | tf_op jit(solution)/shard_map/ppermute | solution.py:23
  48.3 179.8 %collective-permute-start.4 = (f32[1024,256]{1,0:T(8,128)S(1)}, f32[1024,256]{1,0:T(8,128)S(1)}, u32[]{:S(2)}, u32[]{:S(2)}) collective-permute-start(f32[1024,256]{1,0:T(8,128)S(1)} %collective-permute-done.2), channel_id=1, source_target_pairs={{0,1},{1,2},{2,3},{3,0},{4,5},{5,6},{6,7},{7,4},{8,9},{9,10},{10,1... | collective-permute-start | bytes 3145736 | tf_op jit(solution)/shard_map/ppermute | solution.py:18
  93.4 179.7 %collective-permute-start.7 = (f32[1024,256]{1,0:T(8,128)}, f32[1024,256]{1,0:T(8,128)S(1)}, u32[]{:S(2)}, u32[]{:S(2)}) collective-permute-start(f32[1024,256]{1,0:T(8,128)} %collective-permute-done.5), channel_id=1, source_target_pairs={{0,1},{1,2},{2,3},{3,0},{4,5},{5,6},{6,7},{7,4},{8,9},{9,10},{10,1... | collective-permute-start | bytes 3145736 | tf_op jit(solution)/shard_map/ppermute | solution.py:18
  285.1 7.2 %copy-start.7 = (f32[2,1024,1024]{2,1,0:T(8,128)S(1)}, f32[2,1024,1024]{2,1,0:T(8,128)}, u32[]{:S(2)}) copy-start(f32[2,1024,1024]{2,1,0:T(8,128)} %all-gather.2.cloned.1.call-done) | copy-start | bytes 25165828
  288.5 4.0 copy-start.14
  292.5 1.6 copy-start.2
  293.3 14.3 %copy-start.8 = (f32[1024,256]{0,1:T(8,128)}, f32[1024,256]{0,1:T(8,128)S(1)}, u32[]{:S(2)}) copy-start(f32[1024,256]{0,1:T(8,128)S(1)} %fusion.69) | copy-start | bytes 3145732
  299.0 4.9 %copy-start.15 = (f32[1024,256]{0,1:T(8,128)}, f32[1024,256]{0,1:T(8,128)S(1)}, u32[]{:S(2)}) copy-start(f32[1024,256]{0,1:T(8,128)S(1)} %fusion.67) | copy-start | bytes 3145732
  300.6 14.4 %collective-permute-start.9 = (f32[1024,128]{0,1:T(8,128)}, f32[1024,128]{0,1:T(8,128)S(1)}, u32[]{:S(2)}, u32[]{:S(2)}) collective-permute-start(f32[1024,128]{0,1:T(8,128)} %fusion.74), channel_id=1, source_target_pairs={{4,0},{8,4},{12,8},{5,1},{9,5},{13,9},{6,2},{10,6},{14,10},{7,3},{... | collective-permute-start | bytes 1572872 | tf_op jit(solution)/shard_map/ppermute | solution.py:33
  305.5 11.5 %collective-permute-start.8 = (f32[1024,128]{0,1:T(8,128)}, f32[1024,128]{0,1:T(8,128)S(1)}, u32[]{:S(2)}, u32[]{:S(2)}) collective-permute-start(f32[1024,128]{0,1:T(8,128)} %fusion.75), channel_id=1, source_target_pairs={{4,0},{8,4},{12,8},{5,1},{9,5},{13,9},{6,2},{10,6},{14,10},{7,3},{... | collective-permute-start | bytes 1572872 | tf_op jit(solution)/shard_map/ppermute | solution.py:33
  317.0 2.5 copy-start.5
  319.4 1.6 copy-start
  319.4 1.7 copy-start.11
  322.7 1.6 copy-start.3
  322.7 1.7 copy-start.12
  326.0 10.7 %collective-permute-start.1 = (f32[1024,128]{0,1:T(8,128)}, f32[1024,128]{0,1:T(8,128)S(1)}, u32[]{:S(2)}, u32[]{:S(2)}) collective-permute-start(f32[1024,128]{0,1:T(8,128)} %fusion.225), channel_id=1, source_target_pairs={{4,0},{8,4},{12,8},{5,1},{9,5},{13,9},{6,2},{10,6},{14,10},{7,3},{... | collective-permute-start | bytes 1572872 | tf_op jit(solution)/shard_map/while/body/eval_jaxpr/ppermute | solution.py:33
  334.0 10.7 %collective-permute-start = (f32[1024,128]{0,1:T(8,128)}, f32[1024,128]{0,1:T(8,128)S(1)}, u32[]{:S(2)}, u32[]{:S(2)}) collective-permute-start(f32[1024,128]{0,1:T(8,128)} %fusion.219), channel_id=1, source_target_pairs={{4,0},{8,4},{12,8},{5,1},{9,5},{13,9},{6,2},{10,6},{14,10},{7,3},{... | collective-permute-start | bytes 1572872 | tf_op jit(solution)/shard_map/while/body/eval_jaxpr/ppermute | solution.py:33
  344.7 2.5 copy-start.5
  347.2 1.6 copy-start
  347.2 1.7 copy-start.11
  350.4 1.6 copy-start.3
  350.4 1.7 copy-start.12
  353.8 10.7 %collective-permute-start.1 = (f32[1024,128]{0,1:T(8,128)}, f32[1024,128]{0,1:T(8,128)S(1)}, u32[]{:S(2)}, u32[]{:S(2)}) collective-permute-start(f32[1024,128]{0,1:T(8,128)} %fusion.225), channel_id=1, source_target_pairs={{4,0},{8,4},{12,8},{5,1},{9,5},{13,9},{6,2},{10,6},{14,10},{7,3},{... | collective-permute-start | bytes 1572872 | tf_op jit(solution)/shard_map/while/body/eval_jaxpr/ppermute | solution.py:33
  361.7 10.7 %collective-permute-start = (f32[1024,128]{0,1:T(8,128)}, f32[1024,128]{0,1:T(8,128)S(1)}, u32[]{:S(2)}, u32[]{:S(2)}) collective-permute-start(f32[1024,128]{0,1:T(8,128)} %fusion.219), channel_id=1, source_target_pairs={{4,0},{8,4},{12,8},{5,1},{9,5},{13,9},{6,2},{10,6},{14,10},{7,3},{... | collective-permute-start | bytes 1572872 | tf_op jit(solution)/shard_map/while/body/eval_jaxpr/ppermute | solution.py:33
  372.5 2.6 copy-start.1
  376.3 1.6 copy-start.4
  379.9 1.6 copy-start.6
  (7 other events, 7.5 us)
Sparse Core Ops, SparseCore 0:
  8.9 276.1 all-gather.1
